TPU v7x, 256 devices: a whole 4x4x8 slice. The times are simulated.
256 devices in a mesh: var: 8 (over y, core), tok: 32 (over x, z).
Axes of the slice: x: 4, y: 4, z: 8, core: 2. Of those that a mesh axis runs over, the one named last changes fastest.
Arguments:
- patches: bfloat16 [72, 4, 4096], P('var', None, 'tok'), may hold values from -6 to 6
- slot_var: int32 [72], replicated, may hold values from -1 to 47, as said below
- patch_weight: bfloat16 [48, 4, 1024], replicated, may hold values from -3 to 3
- var_embed: bfloat16 [48, 1024], replicated, may hold values from -6 to 6
- query: bfloat16 [1024], replicated, may hold values from -16 to 16
- key_weight: bfloat16 [1024, 1024], P('tok'), may hold values from -0.1875 to 0.1875
- value_weight: bfloat16 [1024, 1024], P('tok'), may hold values from -0.1875 to 0.1875
- out_weight: bfloat16 [1024, 1024], P('tok'), may hold values from -0.1875 to 0.1875
- cotangent: bfloat16 [4096, 1024], P(('tok', 'var')), may hold values from -6 to 6
Outputs:
- aggregated: bfloat16 [4096, 1024], P(('tok', 'var'))
- patch_grad: float32 [72, 4096], P('var', 'tok')
Inputs may be any that keep to these rules, and one draw needn't show every extreme that they name: `slot_var`: slot 9 * i + j belongs to index i of var. Every variable id stands in exactly one slot; empty slots hold -1. The live slots of an index come first and hold consecutive ids, rising from index to index. Every index holds at least one and at most 9 live slots, and some index holds exactly 9.
All inputs are finite; a program needn't handle non-finite values.
Results may differ from a plain program's by a relative error of at most 0.011.
Values may be sent and summed in bfloat16 or wider, within the bound.
No kernel may reach another device: no remote copies, remote signals or barrier semaphores. Data moves between devices by JAX's collectives and lax.ppermute only.
A program may use at most 128 MiB of HBM per device.

v0:
```python
import math
import jax
import jax.numpy as jnp
from jax import lax
from jax.sharding import PartitionSpec as P

H = 16
HD = 64
score_cap = 5.0
inv_sqrt_two = 1.0 / math.sqrt(2.0)
inv_sqrt_two_pi = 1.0 / math.sqrt(2.0 * math.pi)
f32 = jnp.float32
bf16 = jnp.bfloat16


def gelu_exact(inputs):
    return 0.5 * inputs * (1.0 + lax.erf(inputs * inv_sqrt_two))


def gelu_slope(inputs):
    return (
        0.5 * (1.0 + lax.erf(inputs * inv_sqrt_two))
        + inputs * jnp.exp(-0.5 * inputs * inputs) * inv_sqrt_two_pi
    )


def live_index(slot_var, var_total):
    ids = jnp.arange(var_total, dtype=jnp.int32)
    places = jnp.arange(slot_var.shape[0], dtype=jnp.int32)
    match = slot_var[None, :] == ids[:, None]
    return jnp.sum(jnp.where(match, places[None, :], 0), axis=1)


def split(x):
    hi = x.astype(bf16)
    lo = (x - hi.astype(f32)).astype(bf16)
    return (hi, lo)


def ein(spec, a, b):
    return jnp.einsum(spec, a, b, preferred_element_type=f32)


def body(
    patches,
    slot_var,
    patch_weight,
    var_embed,
    query,
    key_weight,
    value_weight,
    out_weight,
    cotangent,
    *,
    n_var,
    n_tok
):
    var_total, pixels_per, width = patch_weight.shape
    local_slots = patches.shape[0]
    rows = key_weight.shape[0]
    tok_count = cotangent.shape[0]
    query_heads = query.reshape(H, HD).astype(f32)
    wq_rows = jnp.sum(key_weight.reshape(rows, H, HD).astype(f32) * query_heads[None], axis=2)
    wq_copies = jnp.broadcast_to(wq_rows[None], (n_tok, rows, H))
    wq_full = lax.all_to_all(wq_copies, "tok", 0, 0, tiled=True).reshape(n_tok * rows, H)
    wq_hi, wq_lo = split(wq_full)
    full = lax.all_gather(jnp.stack([value_weight, out_weight]), "tok", axis=1, tiled=True)
    value_matrix = full[0]
    out_matrix = full[1]
    slot_pixels = lax.all_to_all(patches, "var", 2, 0, tiled=True)
    live_slot = live_index(slot_var, var_total)
    pixels = jnp.take(slot_pixels, live_slot, axis=0)
    pre_act = ein("vpt,vpd->vtd", pixels, patch_weight) + var_embed.astype(f32)[:, None, :]
    embedded = gelu_exact(pre_act).astype(bf16)
    raw_scores = (
        ein("vtd,dh->tvh", embedded, wq_hi) + ein("vtd,dh->tvh", embedded, wq_lo)
    ) / math.sqrt(HD)
    squashed = jnp.tanh(raw_scores / score_cap)
    exp_scores = jnp.exp(score_cap * squashed)
    attn_f32 = exp_scores / jnp.sum(exp_scores, axis=1, keepdims=True)
    attn_bf = attn_f32.astype(bf16)
    value_heads = value_matrix.reshape(width, H, HD)
    mixed_in = ein("tvh,vtd->thd", attn_bf, embedded)
    mix_hi, mix_lo = split(mixed_in)
    pooled = (
        (ein("thd,dhj->thj", mix_hi, value_heads) + ein("thd,dhj->thj", mix_lo, value_heads))
        .astype(bf16)
        .reshape(tok_count, width)
    )
    mixed_out = jnp.dot(pooled, out_matrix, preferred_element_type=f32).astype(bf16)
    contract = (((1,), (1,)), ((), ()))
    grad_pooled = (
        lax.dot_general(cotangent, out_matrix, contract, preferred_element_type=f32)
        .astype(bf16)
        .reshape(tok_count, H, HD)
    )
    spread = ein("thj,dhj->thd", grad_pooled, value_heads)
    spread_hi, spread_lo = split(spread)
    grad_attn = ein("vtd,thd->tvh", embedded, spread_hi) + ein("vtd,thd->tvh", embedded, spread_lo)
    grad_scores = attn_f32 * (grad_attn - jnp.sum(attn_f32 * grad_attn, axis=1, keepdims=True))
    grad_raw = grad_scores * (1.0 - squashed * squashed) / math.sqrt(HD)
    raw_hi, raw_lo = split(grad_raw)
    grad_embed = (
        ein("tvh,thd->vtd", attn_bf, spread_hi)
        + ein("tvh,thd->vtd", attn_bf, spread_lo)
        + ein("tvh,dh->vtd", raw_hi, wq_hi)
        + ein("tvh,dh->vtd", raw_hi, wq_lo)
        + ein("tvh,dh->vtd", raw_lo, wq_hi)
    ).astype(bf16)
    grad_pre = grad_embed.astype(f32) * gelu_slope(pre_act)
    partial = jnp.einsum(
        "vpt,vtd->vpd", pixels.astype(f32), grad_pre, precision=lax.Precision.HIGHEST
    ).reshape(var_total, pixels_per * width)
    slots = n_var * local_slots
    cols = partial.shape[1] // n_tok
    safe = jnp.clip(slot_var, 0, var_total - 1)
    slot_rows = jnp.where((slot_var >= 0)[:, None], jnp.take(partial, safe, axis=0), 0.0)
    blocks = slot_rows.reshape(n_var, local_slots, n_tok, cols).transpose(0, 2, 1, 3)
    by_var = lax.all_to_all(blocks, "var", 0, 0, tiled=True).sum(axis=0)
    by_tok = lax.all_to_all(by_var, "tok", 0, 0, tiled=True).sum(axis=0)
    del slots
    return (mixed_out, by_tok)


def solution(mesh):
    import functools

    fn = functools.partial(body, n_var=mesh.shape["var"], n_tok=mesh.shape["tok"])
    return jax.shard_map(
        fn,
        mesh=mesh,
        in_specs=(
            P("var", None, "tok"),
            P(),
            P(),
            P(),
            P(),
            P("tok", None),
            P("tok", None),
            P("tok", None),
            P(("tok", "var"), None),
        ),
        out_specs=(P(("tok", "var"), None), P("var", "tok")),
        check_vma=False,
    )
```

profile of v0, /device:TPU:32, one launch (start us, length us, event | category | flops | bytes accessed | tf_op | source)
XLA Modules:
  0.0 189.6 jit_solution(7815867198240021874)
XLA Ops:
  10.5 4.5 %all-to-all-start.1 = ((bf16[8,2,288]{2,1,0:T(2,128)(2,1)}), bf16[8,2,288]{2,1,0:T(2,128)(2,1)S(1)}, u32[]{:S(2)}, u32[]{:S(2)}) async-start(bf16[8,2,288]{2,1,0:T(2,128)(2,1)} %reshape.93), calls=%async_computation.1 | async-start | bytes 24576 | tf_op jit(solution)/shard_map/all_to_all | solution.py:70
  20.9 11.2 %all-to-all-start = ((f32[32,1,512]{2,1,0:T(1,128)}), f32[32,1,512]{2,1,0:T(1,128)S(1)}, u32[]{:S(2)}, u32[]{:S(2)}) async-start(f32[32,1,512]{2,1,0:T(1,128)} %reshape.95), calls=%async_computation | async-start | bytes 131072 | tf_op jit(solution)/shard_map/all_to_all | solution.py:65
  33.4 2.9 %multiply_convert_fusion = (bf16[48,16,1024]{2,1,0:T(8,128)(2,1)S(1)}, f32[48,16,1024]{2,1,0:T(8,128)}) fusion(f32[48,1024]{1,0:T(8,128)S(1)} %convert_element_type.88, bf16[48,4,1024]{2,1,0:T(4,128)(2,1)S(1)} %copy-done, bf16[48,4,16]{2,1,0:T(4,128)(2,1)S(1)} %gather_fusion, pred[48]{0:T(512)(128)(4,1)S(1)} %compare_and_fusion.1), kind=kOutput, calls=%fused_computation.17 | convolution fusion | flops 11013120 | bytes 5314608 | tf_op jit(solution)/shard_map/vpt,vpd->vtd/dot_general | solution.py:41
  36.4 5.1 %all-to-all-done = f32[32,1,512]{2,1,0:T(1,128)S(1)} async-done(((f32[32,1,512]{2,1,0:T(1,128)}), f32[32,1,512]{2,1,0:T(1,128)S(1)}, u32[]{:S(2)}, u32[]{:S(2)}) %all-to-all-start) | async-done | bytes 65568 | tf_op jit(solution)/shard_map/all_to_all | solution.py:65
  46.6 48.1 %all-gather.2.cloned.1.call-done = bf16[2,1024,1024]{2,1,0:T(8,128)(2,1)} async-done(((bf16[2,32,1024]{2,1,0:T(8,128)(2,1)}), bf16[2,1024,1024]{2,1,0:T(8,128)(2,1)}) %all-gather.2.cloned.1.call-update) | async-done | bytes 4194320 | tf_op jit(solution)/shard_map/all_gather | solution.py:67
  94.7 3.1 %slice.12 = bf16[1,1024,1024]{2,1,0:T(8,128)(2,1)} slice(bf16[2,1024,1024]{2,1,0:T(8,128)(2,1)} %all-gather.2.cloned.1.call-done), slice={[0:1], [0:1024], [0:1024]} | slice | bytes 4194304 | tf_op jit(solution)/shard_map/slice | solution.py:68
  97.8 3.0 %copy.107 = bf16[1,1024,1024]{1,2,0:T(8,128)(2,1)S(1)} copy(bf16[1,1024,1024]{2,1,0:T(8,128)(2,1)} %slice.12) | data formatting | bytes 4194304 | tf_op jit(solution)/shard_map/slice | solution.py:68
  100.9 2.2 %fusion.28 = bf16[16,1024]{1,0:T(8,128)(2,1)S(1)} fusion(bf16[16,1024]{1,0:T(8,128)(2,1)S(1)} %copy-done.20, bf16[2,1024,1024]{2,1,0:T(8,128)(2,1)} %all-gather.2.cloned.1.call-done), kind=kOutput, calls=%fused_computation.42 | convolution fusion | flops 33570816 | bytes 2162688 | tf_op jit(solution)/shard_map/dot_general | solution.py:93
  106.8 2.6 %convolution_add_fusion.2 = f32[16,48,16]{1,2,0:T(8,128)S(1)} fusion(f32[16,48,16]{1,2,0:T(8,128)S(1)} %fusion.30, bf16[48,16,1024]{2,1,0:T(8,128)(2,1)S(1)} %copy-done.2, bf16[16,16,1024]{2,0,1:T(8,128)(2,1)S(1)} %get-tuple-element.8), kind=kOutput, calls=%fused_computation.37 | convolution fusion | flops 25178112 | bytes 2195456 | tf_op jit(solution)/shard_map/vtd,thd->tvh/dot_general | solution.py:41
  109.4 1.9 %subtract_convert_fusion.2 = (bf16[16,48,16]{1,2,0:T(8,128)(2,1)}, bf16[16,48,16]{1,2,0:T(8,128)(2,1)}) fusion(f32[16,48,16]{1,0,2:T(8,128)S(1)} %copy-done.15, f32[16,48,16]{1,2,0:T(8,128)S(1)} %convolution_add_fusion.2, f32[16,16]{1,0:T(8,128)S(1)} %get-tuple-element.13), kind=kOutput, calls=%fused_computation.67 | output fusion | flops 184623 | bytes 148480 | tf_op jit(solution)/shard_map/sub | solution.py:100
  111.3 1.7 copy.128
  113.0 3.3 %fusion.56 = f32[1024,16,48]{0,1,2:T(8,128)} fusion(bf16[16,48,16]{2,0,1:T(8,128)(2,1)} %copy.128, f32[1024,16]{0,1:T(8,128)} %copy-done.5), kind=kOutput, calls=%fused_computation.84 | convolution fusion | flops 25231360 | bytes 3235840 | tf_op jit(solution)/shard_map/tvh,dh->vtd/dot_general | solution.py:41
  116.4 2.3 %fusion.50 = f32[1024,16,48]{0,1,2:T(8,128)} fusion(bf16[16,48,16]{2,0,1:T(8,128)(2,1)S(1)} %copy-done.4, f32[1024,16]{0,1:T(8,128)S(1)} %copy-done.6), kind=kOutput, calls=%fused_computation.76 | convolution fusion | flops 25182208 | bytes 3235840 | tf_op jit(solution)/shard_map/tvh,dh->vtd/dot_general | solution.py:41
  118.7 2.2 %fusion.41 = f32[16,1024,48]{1,2,0:T(8,128)} fusion(bf16[16,48,16]{1,2,0:T(8,128)(2,1)S(1)} %copy-done.8, bf16[16,16,1024]{2,0,1:T(8,128)(2,1)S(1)} %get-tuple-element.8), kind=kOutput, calls=%fused_computation.57 | convolution fusion | flops 25165824 | bytes 3694592 | tf_op jit(solution)/shard_map/tvh,thd->vtd/dot_general | solution.py:41
  120.9 2.3 %fusion.44 = f32[16,1024,48]{1,2,0:T(8,128)} fusion(bf16[16,48,16]{1,2,0:T(8,128)(2,1)S(1)} %copy-done.8, bf16[16,16,1024]{2,0,1:T(8,128)(2,1)S(1)} %get-tuple-element.9), kind=kOutput, calls=%fused_computation.60 | convolution fusion | flops 25165824 | bytes 3694592 | tf_op jit(solution)/shard_map/tvh,thd->vtd/dot_general | solution.py:41
  123.4 8.5 %fusion.8 = bf16[48,16,1024]{2,1,0:T(8,128)(2,1)S(1)} fusion(f32[1024,16,48]{0,1,2:T(8,128)} %fusion.56, f32[1024,16,48]{0,1,2:T(8,128)} %fusion.50, f32[16,1024,48]{1,2,0:T(8,128)} %fusion.41, f32[16,1024,48]{1,2,0:T(8,128)} %fusion.44, bf16[16,48,16]{2,0,1:T(8,128)(2,1)S(1)} %copy.130, f32[1024,16]{0,1:T(8,128)S(1)} %copy-done.7), kind=kOutput, calls=%fused_computation.11 | convolution fusion | flops 29114368 | bytes 14245888 | tf_op jit(solution)/shard_map/tvh,dh->vtd/dot_general | solution.py:41
  131.9 3.2 %fusion.6 = f32[48,4,1024]{2,1,0:T(4,128)S(1)} fusion(bf16[48,16,1024]{2,1,0:T(8,128)(2,1)S(1)} %fusion.8, f32[48,16,1024]{2,1,0:T(8,128)S(1)} %copy-done.3, f32[48,1024]{1,0:T(8,128)S(1)} %copy-done.11, bf16[48,4,16]{2,1,0:T(4,128)(2,1)S(1)} %copy-done.13, pred[48]{0:T(512)(128)(4,1)S(1)} %copy-done.19), kind=kOutput, calls=%fused_computation.9 | convolution fusion | flops 46402560 | bytes 5707824 | tf_op jit(solution)/shard_map/vpt,vtd->vpd/dot_general | solution.py:111
  135.6 2.0 %gather_fusion.1 = f32[72,4096]{1,0:T(8,128)} fusion(f32[48,4096]{1,0:T(8,128)S(1)} %bitcast.98, s32[1024]{0:T(1024)S(1)} %pad_clamp_fusion), kind=kCustom, calls=%fused_computation.1 | custom fusion | bytes 2359584 | tf_op jit(solution)/shard_map/jit(_take)/gather | solution.py:117
  140.4 4.3 %all-to-all-start.2 = ((f32[8,32,9,128]{3,1,2,0:T(8,128)}), f32[8,32,9,128]{3,1,2,0:T(8,128)}, u32[]{:S(2)}, u32[]{:S(2)}) async-start(f32[8,32,9,128]{3,1,2,0:T(8,128)} %select_bitcast_fusion), calls=%async_computation.2 | async-start | bytes 2359296 | tf_op jit(solution)/shard_map/all_to_all | solution.py:119
  144.7 3.2 %subtract_convert_fusion.1 = (bf16[16,16,1024]{2,1,0:T(8,128)(2,1)S(1)}, bf16[16,16,1024]{2,1,0:T(8,128)(2,1)S(1)}) fusion(bf16[16,48,16]{1,2,0:T(8,128)(2,1)S(1)} %copy-done.9, bf16[48,16,1024]{2,1,0:T(8,128)(2,1)} %copy-done.1), kind=kOutput, calls=%fused_computation.44 | convolution fusion | flops 26214400 | bytes 2646016 | tf_op jit(solution)/shard_map/tvh,vtd->thd/dot_general | solution.py:41
  148.5 13.6 %all-to-all-done.2 = f32[8,32,9,128]{3,1,2,0:T(8,128)} async-done(((f32[8,32,9,128]{3,1,2,0:T(8,128)}), f32[8,32,9,128]{3,1,2,0:T(8,128)}, u32[]{:S(2)}, u32[]{:S(2)}) %all-to-all-start.2) | async-done | bytes 1179680 | tf_op jit(solution)/shard_map/all_to_all | solution.py:119
  164.3 5.8 %all-to-all-start.3 = ((f32[32,9,128]{2,1,0:T(8,128)}), f32[32,9,128]{2,1,0:T(8,128)S(1)}, u32[]{:S(2)}, u32[]{:S(2)}) async-start(f32[32,9,128]{2,1,0:T(8,128)} %copy.131), calls=%async_computation.3 | async-start | bytes 524288 | tf_op jit(solution)/shard_map/all_to_all | solution.py:120
  170.9 2.6 %fusion.26 = bf16[16,1024]{1,0:T(8,128)(2,1)} fusion(bf16[16,1024]{1,0:T(8,128)(2,1)S(1)} %reshape.69, bf16[2,1024,1024]{2,1,0:T(8,128)(2,1)} %all-gather.2.cloned.1.call-done), kind=kOutput, calls=%fused_computation.40 | convolution fusion | flops 33570816 | bytes 2162688 | tf_op jit(solution)/shard_map/dot_general | solution.py:90
  173.5 8.6 %all-to-all-done.3 = f32[32,9,128]{2,1,0:T(8,128)S(1)} async-done(((f32[32,9,128]{2,1,0:T(8,128)}), f32[32,9,128]{2,1,0:T(8,128)S(1)}, u32[]{:S(2)}, u32[]{:S(2)}) %all-to-all-start.3) | async-done | bytes 147488 | tf_op jit(solution)/shard_map/all_to_all | solution.py:120
  (89 shorter events, 27.0 us)
Async XLA Ops:
  7.2 26.2 %copy-start = (bf16[48,4,1024]{2,1,0:T(4,128)(2,1)S(1)}, bf16[48,4,1024]{2,1,0:T(4,128)(2,1)}, u32[]{:S(2)}) copy-start(bf16[48,4,1024]{2,1,0:T(4,128)(2,1)} %param.11) | copy-start | bytes 1179652
  7.2 87.5 %all-gather.2.cloned.1.call-start = ((), (), s32[]{:S(2)}) async-start(), calls=%async_computation.4 | async-start | bytes 4325376 | tf_op jit(solution)/shard_map/all_gather | solution.py:67
  10.5 10.4 %all-to-all-start.1 = ((bf16[8,2,288]{2,1,0:T(2,128)(2,1)}), bf16[8,2,288]{2,1,0:T(2,128)(2,1)S(1)}, u32[]{:S(2)}, u32[]{:S(2)}) async-start(bf16[8,2,288]{2,1,0:T(2,128)(2,1)} %reshape.93), calls=%async_computation.1 | async-start | bytes 24576 | tf_op jit(solution)/shard_map/all_to_all | solution.py:70
  17.7 18.6 %copy-start.18 = (pred[48]{0:T(512)(128)(4,1)}, pred[48]{0:T(512)(128)(4,1)S(1)}, u32[]{:S(2)}) copy-start(pred[48]{0:T(512)(128)(4,1)S(1)} %compare_and_fusion.1) | copy-start | bytes 148
  19.3 17.0 %copy-start.10 = (f32[48,1024]{1,0:T(8,128)}, f32[48,1024]{1,0:T(8,128)S(1)}, u32[]{:S(2)}) copy-start(f32[48,1024]{1,0:T(8,128)S(1)} %convert_element_type.88) | copy-start | bytes 589828
  20.9 20.6 %all-to-all-start = ((f32[32,1,512]{2,1,0:T(1,128)}), f32[32,1,512]{2,1,0:T(1,128)S(1)}, u32[]{:S(2)}, u32[]{:S(2)}) async-start(f32[32,1,512]{2,1,0:T(1,128)} %reshape.95), calls=%async_computation | async-start | bytes 131072 | tf_op jit(solution)/shard_map/all_to_all | solution.py:65
  33.4 8.0 %copy-start.12 = (bf16[48,4,16]{2,1,0:T(4,128)(2,1)}, bf16[48,4,16]{2,1,0:T(4,128)(2,1)S(1)}, u32[]{:S(2)}) copy-start(bf16[48,4,16]{2,1,0:T(4,128)(2,1)S(1)} %gather_fusion) | copy-start | bytes 18436
  36.4 58.3 %copy-start.1 = (bf16[48,16,1024]{2,1,0:T(8,128)(2,1)}, bf16[48,16,1024]{2,1,0:T(8,128)(2,1)S(1)}, u32[]{:S(2)}) copy-start(bf16[48,16,1024]{2,1,0:T(8,128)(2,1)S(1)} %get-tuple-element.11) | copy-start | bytes 4718596
  43.1 51.6 %copy-start.5 = (f32[1024,16]{0,1:T(8,128)}, f32[1024,16]{0,1:T(8,128)S(1)}, u32[]{:S(2)}) copy-start(f32[1024,16]{0,1:T(8,128)S(1)} %reshape.68) | copy-start | bytes 196612
  46.6 54.3 %copy-start.20 = (bf16[16,1024]{1,0:T(8,128)(2,1)S(1)}, bf16[16,1024]{1,0:T(8,128)(2,1)}, u32[]{:S(2)}) copy-start(bf16[16,1024]{1,0:T(8,128)(2,1)} %param.17) | copy-start | bytes 98308
  105.2 4.2 %copy-start.15 = (f32[16,48,16]{1,0,2:T(8,128)S(1)}, f32[16,48,16]{1,0,2:T(8,128)}, u32[]{:S(2)}) copy-start(f32[16,48,16]{1,0,2:T(8,128)} %copy-done.14) | copy-start | bytes 147460
  113.0 3.3 %copy-start.4 = (bf16[16,48,16]{2,0,1:T(8,128)(2,1)S(1)}, bf16[16,48,16]{2,0,1:T(8,128)(2,1)}, u32[]{:S(2)}) copy-start(bf16[16,48,16]{2,0,1:T(8,128)(2,1)} %copy.128) | copy-start | bytes 73732
  113.0 3.3 %copy-start.6 = (f32[1024,16]{0,1:T(8,128)S(1)}, f32[1024,16]{0,1:T(8,128)}, u32[]{:S(2)}) copy-start(f32[1024,16]{0,1:T(8,128)} %copy-done.5) | copy-start | bytes 196612
  113.0 5.6 %copy-start.8 = (bf16[16,48,16]{1,2,0:T(8,128)(2,1)S(1)}, bf16[16,48,16]{1,2,0:T(8,128)(2,1)}, u32[]{:S(2)}) copy-start(bf16[16,48,16]{1,2,0:T(8,128)(2,1)} %fusion.59) | copy-start | bytes 73732
  120.9 2.3 %copy-start.16 = (bf16[16,48,16]{1,2,0:T(8,128)(2,1)S(1)}, bf16[16,48,16]{1,2,0:T(8,128)(2,1)}, u32[]{:S(2)}) copy-start(bf16[16,48,16]{1,2,0:T(8,128)(2,1)} %get-tuple-element.4) | copy-start | bytes 73732
  120.9 2.5 %copy-start.7 = (f32[1024,16]{0,1:T(8,128)S(1)}, f32[1024,16]{0,1:T(8,128)}, u32[]{:S(2)}) copy-start(f32[1024,16]{0,1:T(8,128)} %copy-done.5) | copy-start | bytes 196612
  123.4 8.5 %copy-start.3 = (f32[48,16,1024]{2,1,0:T(8,128)S(1)}, f32[48,16,1024]{2,1,0:T(8,128)}, u32[]{:S(2)}) copy-start(f32[48,16,1024]{2,1,0:T(8,128)} %get-tuple-element.12) | copy-start | bytes 9437188
  123.4 8.5 %copy-start.11 = (f32[48,1024]{1,0:T(8,128)S(1)}, f32[48,1024]{1,0:T(8,128)}, u32[]{:S(2)}) copy-start(f32[48,1024]{1,0:T(8,128)} %copy-done.10) | copy-start | bytes 589828
  123.4 8.5 %copy-start.13 = (bf16[48,4,16]{2,1,0:T(4,128)(2,1)S(1)}, bf16[48,4,16]{2,1,0:T(4,128)(2,1)}, u32[]{:S(2)}) copy-start(bf16[48,4,16]{2,1,0:T(4,128)(2,1)} %copy-done.12) | copy-start | bytes 18436
  123.4 8.5 %copy-start.19 = (pred[48]{0:T(512)(128)(4,1)S(1)}, pred[48]{0:T(512)(128)(4,1)}, u32[]{:S(2)}) copy-start(pred[48]{0:T(512)(128)(4,1)} %copy-done.18) | copy-start | bytes 148
  135.6 3.5 %copy-start.17 = (pred[8,9]{1,0:T(8,128)(4,1)S(1)}, pred[8,9]{1,0:T(8,128)(4,1)}, u32[]{:S(2)}) copy-start(pred[8,9]{1,0:T(8,128)(4,1)} %broadcast_in_dim.69) | copy-start | bytes 220
  137.6 7.1 %copy-start.9 = (bf16[16,48,16]{1,2,0:T(8,128)(2,1)S(1)}, bf16[16,48,16]{1,2,0:T(8,128)(2,1)}, u32[]{:S(2)}) copy-start(bf16[16,48,16]{1,2,0:T(8,128)(2,1)} %fusion.59) | copy-start | bytes 73732
  140.4 21.7 %all-to-all-start.2 = ((f32[8,32,9,128]{3,1,2,0:T(8,128)}), f32[8,32,9,128]{3,1,2,0:T(8,128)}, u32[]{:S(2)}, u32[]{:S(2)}) async-start(f32[8,32,9,128]{3,1,2,0:T(8,128)} %select_bitcast_fusion), calls=%async_computation.2 | async-start | bytes 2359296 | tf_op jit(solution)/shard_map/all_to_all | solution.py:119
  164.3 17.8 %all-to-all-start.3 = ((f32[32,9,128]{2,1,0:T(8,128)}), f32[32,9,128]{2,1,0:T(8,128)S(1)}, u32[]{:S(2)}, u32[]{:S(2)}) async-start(f32[32,9,128]{2,1,0:T(8,128)} %copy.131), calls=%async_computation.3 | async-start | bytes 524288 | tf_op jit(solution)/shard_map/all_to_all | solution.py:120
  (2 other events, 2.1 us)
Sparse Core Ops, SparseCore 0:
  10.6 84.0 all-gather.1
where the time goes:
time: 190 us
  waiting for transfers between devices  75.3 us (40%)
  matrix products  41.6 us (22%)
  starting transfers between devices  25.8 us (14%)
  local copies, waits for them, and re-layouts  21.7 us (11%)
  between operations  14.4 us (8%)
  other arithmetic  10.8 us (6%)
    all_gather x1, waiting for transfers between devices, body(): lax.all_gather(jnp.stack([value_weight, out_weight]), 'tok', axis=1, tile...  48.1 us
    dot_general x14, matrix products, ein(): return jnp.einsum(spec, a, b, preferred_element_type=f32)  33.6 us
    all_to_all x1, waiting for transfers between devices, body(): by_var = lax.all_to_all(blocks, 'var', 0, 0, tiled=True).sum(axis=0)  13.6 us
    all_to_all x1, starting transfers between devices, body(): lax.all_to_all(wq_copies, 'tok', 0, 0, tiled=True).reshape(n_tok * rows, H)  11.2 us
    all_to_all x1, waiting for transfers between devices, body(): by_tok = lax.all_to_all(by_var, 'tok', 0, 0, tiled=True).sum(axis=0)  8.57 us
    slice x2, local copies, waits for them, and re-layouts, body(): value_matrix = full[0]  6.18 us
    all_to_all x1, starting transfers between devices, body(): by_tok = lax.all_to_all(by_var, 'tok', 0, 0, tiled=True).sum(axis=0)  5.8 us
    unnamed x50, local copies, waits for them, and re-layouts  5.65 us
  transfers between devices with their start and end apart: 5, of which 4 were waited for; matrix products, arithmetic and copies ran while one was open for 12% of the time, Pallas kernels for 0%

commit v1 on v0

--- a/solution.py
+++ b/solution.py
@@ -67,7 +67,9 @@
     full = lax.all_gather(jnp.stack([value_weight, out_weight]), "tok", axis=1, tiled=True)
     value_matrix = full[0]
     out_matrix = full[1]
-    slot_pixels = lax.all_to_all(patches, "var", 2, 0, tiled=True)
+    cells = jnp.split(patches, lax.axis_size("var"), axis=2)
+    received = lax.all_to_all(jnp.stack(cells), "var", 0, 0)
+    slot_pixels = jnp.concatenate(received, axis=0)
     live_slot = live_index(slot_var, var_total)
     pixels = jnp.take(slot_pixels, live_slot, axis=0)
     pre_act = ein("vpt,vpd->vtd", pixels, patch_weight) + var_embed.astype(f32)[:, None, :]

time: 190 us -> 191 us (level)
  waiting for transfers between devices: 75.3 us -> 70.6 us
  local copies, waits for them, and re-layouts: 21.7 us -> 26.4 us
    all_gather x1, waiting for transfers between devices: 48.1 us -> 42.5 us  [body(): lax.all_gather(jnp.stack([value_weight, out_weight]), 'tok', axis=1, tile...]
    unnamed x50 -> x56, local copies, waits for them, and re-layouts: 5.65 us -> 9.95 us
  transfers between devices with their start and end apart: 5 -> 5, of which waited for: 4 -> 4; matrix products, arithmetic and copies ran while one was open for 12% -> 15% of each run, Pallas kernels for 0% -> 0%
where the time goes in v1:
time: 191 us; the launch traced here: 190 us
  waiting for transfers between devices  70.6 us (37%)
  matrix products  41.6 us (22%)
  local copies, waits for them, and re-layouts  26.4 us (14%)
  starting transfers between devices  25.8 us (14%)
  between operations  14.4 us (8%)
  other arithmetic  10.8 us (6%)
    all_gather x1, waiting for transfers between devices, body(): lax.all_gather(jnp.stack([value_weight, out_weight]), 'tok', axis=1, tile...  42.5 us
    dot_general x14, matrix products, ein(): return jnp.einsum(spec, a, b, preferred_element_type=f32)  33.6 us
    all_to_all x1, waiting for transfers between devices, body(): by_var = lax.all_to_all(blocks, 'var', 0, 0, tiled=True).sum(axis=0)  13.6 us
    all_to_all x1, starting transfers between devices, body(): lax.all_to_all(wq_copies, 'tok', 0, 0, tiled=True).reshape(n_tok * rows, H)  11.2 us
    unnamed x56, local copies, waits for them, and re-layouts  9.95 us
    all_to_all x1, waiting for transfers between devices, body(): by_tok = lax.all_to_all(by_var, 'tok', 0, 0, tiled=True).sum(axis=0)  8.57 us
    slice x2, local copies, waits for them, and re-layouts, body(): value_matrix = full[0]  6.18 us
    all_to_all x1, waiting for transfers between devices, body(): lax.all_to_all(wq_copies, 'tok', 0, 0, tiled=True).reshape(n_tok * rows, H)  5.96 us
  transfers between devices with their start and end apart: 5, of which 4 were waited for; matrix products, arithmetic and copies ran while one was open for 15% of the time, Pallas kernels for 0%

profile of v1, /device:TPU:32, one launch (start us, length us, event | category | flops | bytes accessed | tf_op | source)
XLA Modules:
  0.0 189.6 jit_solution(7799157490378960787)
XLA Ops:
  15.8 4.5 %all-to-all-start.1 = ((bf16[8,2,288]{2,1,0:T(2,128)(2,1)}), bf16[8,2,288]{2,1,0:T(2,128)(2,1)S(1)}, u32[]{:S(2)}, u32[]{:S(2)}) async-start(bf16[8,2,288]{2,1,0:T(2,128)(2,1)} %reshape.97), calls=%async_computation.1 | async-start | bytes 24576 | tf_op jit(solution)/shard_map/all_to_all | solution.py:71
  26.1 11.2 %all-to-all-start = ((f32[32,1,512]{2,1,0:T(1,128)}), f32[32,1,512]{2,1,0:T(1,128)S(1)}, u32[]{:S(2)}, u32[]{:S(2)}) async-start(f32[32,1,512]{2,1,0:T(1,128)} %reshape.99), calls=%async_computation | async-start | bytes 131072 | tf_op jit(solution)/shard_map/all_to_all | solution.py:65
  38.1 2.9 %multiply_convert_fusion = (bf16[48,16,1024]{2,1,0:T(8,128)(2,1)S(1)}, f32[48,16,1024]{2,1,0:T(8,128)}) fusion(f32[48,1024]{1,0:T(8,128)S(1)} %convert_element_type.88, bf16[48,4,1024]{2,1,0:T(4,128)(2,1)S(1)} %copy-done, bf16[48,4,16]{2,1,0:T(4,128)(2,1)S(1)} %gather_fusion, pred[48]{0:T(512)(128)(4,1)S(1)} %compare_and_fusion.1), kind=kOutput, calls=%fused_computation.17 | convolution fusion | flops 11013120 | bytes 5314608 | tf_op jit(solution)/shard_map/vpt,vpd->vtd/dot_general | solution.py:41
  41.1 6.0 %all-to-all-done = f32[32,1,512]{2,1,0:T(1,128)S(1)} async-done(((f32[32,1,512]{2,1,0:T(1,128)}), f32[32,1,512]{2,1,0:T(1,128)S(1)}, u32[]{:S(2)}, u32[]{:S(2)}) %all-to-all-start) | async-done | bytes 65568 | tf_op jit(solution)/shard_map/all_to_all | solution.py:65
  52.2 42.5 %all-gather.2.cloned.1.call-done = bf16[2,1024,1024]{2,1,0:T(8,128)(2,1)} async-done(((bf16[2,32,1024]{2,1,0:T(8,128)(2,1)}), bf16[2,1024,1024]{2,1,0:T(8,128)(2,1)}) %all-gather.2.cloned.1.call-update) | async-done | bytes 4194320 | tf_op jit(solution)/shard_map/all_gather | solution.py:67
  94.7 3.1 %slice.12 = bf16[1,1024,1024]{2,1,0:T(8,128)(2,1)} slice(bf16[2,1024,1024]{2,1,0:T(8,128)(2,1)} %all-gather.2.cloned.1.call-done), slice={[0:1], [0:1024], [0:1024]} | slice | bytes 4194304 | tf_op jit(solution)/shard_map/slice | solution.py:68
  97.8 3.0 %copy.77 = bf16[1,1024,1024]{1,2,0:T(8,128)(2,1)S(1)} copy(bf16[1,1024,1024]{2,1,0:T(8,128)(2,1)} %slice.12) | data formatting | bytes 4194304 | tf_op jit(solution)/shard_map/slice | solution.py:68
  100.9 2.2 %fusion.28 = bf16[16,1024]{1,0:T(8,128)(2,1)S(1)} fusion(bf16[16,1024]{1,0:T(8,128)(2,1)S(1)} %copy-done.20, bf16[2,1024,1024]{2,1,0:T(8,128)(2,1)} %all-gather.2.cloned.1.call-done), kind=kOutput, calls=%fused_computation.42 | convolution fusion | flops 33570816 | bytes 2162688 | tf_op jit(solution)/shard_map/dot_general | solution.py:95
  106.8 2.6 %convolution_add_fusion.2 = f32[16,48,16]{1,2,0:T(8,128)S(1)} fusion(f32[16,48,16]{1,2,0:T(8,128)S(1)} %fusion.30, bf16[48,16,1024]{2,1,0:T(8,128)(2,1)S(1)} %copy-done.2, bf16[16,16,1024]{2,0,1:T(8,128)(2,1)S(1)} %get-tuple-element.8), kind=kOutput, calls=%fused_computation.37 | convolution fusion | flops 25178112 | bytes 2195456 | tf_op jit(solution)/shard_map/vtd,thd->tvh/dot_general | solution.py:41
  109.4 1.9 %subtract_convert_fusion.2 = (bf16[16,48,16]{1,2,0:T(8,128)(2,1)}, bf16[16,48,16]{1,2,0:T(8,128)(2,1)}) fusion(f32[16,48,16]{1,0,2:T(8,128)S(1)} %copy-done.15, f32[16,48,16]{1,2,0:T(8,128)S(1)} %convolution_add_fusion.2, f32[16,16]{1,0:T(8,128)S(1)} %get-tuple-element.13), kind=kOutput, calls=%fused_computation.66 | output fusion | flops 184623 | bytes 148480 | tf_op jit(solution)/shard_map/sub | solution.py:102
  111.3 1.7 copy.95
  113.0 3.3 %fusion.56 = f32[1024,16,48]{0,1,2:T(8,128)} fusion(bf16[16,48,16]{2,0,1:T(8,128)(2,1)} %copy.95, f32[1024,16]{0,1:T(8,128)} %copy-done.5), kind=kOutput, calls=%fused_computation.91 | convolution fusion | flops 25231360 | bytes 3235840 | tf_op jit(solution)/shard_map/tvh,dh->vtd/dot_general | solution.py:41
  116.3 2.3 %fusion.50 = f32[1024,16,48]{0,1,2:T(8,128)} fusion(bf16[16,48,16]{2,0,1:T(8,128)(2,1)S(1)} %copy-done.4, f32[1024,16]{0,1:T(8,128)S(1)} %copy-done.6), kind=kOutput, calls=%fused_computation.75 | convolution fusion | flops 25182208 | bytes 3235840 | tf_op jit(solution)/shard_map/tvh,dh->vtd/dot_general | solution.py:41
  118.7 2.2 %fusion.41 = f32[16,1024,48]{1,2,0:T(8,128)} fusion(bf16[16,48,16]{1,2,0:T(8,128)(2,1)S(1)} %copy-done.8, bf16[16,16,1024]{2,0,1:T(8,128)(2,1)S(1)} %get-tuple-element.8), kind=kOutput, calls=%fused_computation.57 | convolution fusion | flops 25165824 | bytes 3694592 | tf_op jit(solution)/shard_map/tvh,thd->vtd/dot_general | solution.py:41
  120.9 2.3 %fusion.44 = f32[16,1024,48]{1,2,0:T(8,128)} fusion(bf16[16,48,16]{1,2,0:T(8,128)(2,1)S(1)} %copy-done.8, bf16[16,16,1024]{2,0,1:T(8,128)(2,1)S(1)} %get-tuple-element.9), kind=kOutput, calls=%fused_computation.60 | convolution fusion | flops 25165824 | bytes 3694592 | tf_op jit(solution)/shard_map/tvh,thd->vtd/dot_general | solution.py:41
  123.4 8.5 %fusion.8 = bf16[48,16,1024]{2,1,0:T(8,128)(2,1)S(1)} fusion(f32[1024,16,48]{0,1,2:T(8,128)} %fusion.56, f32[1024,16,48]{0,1,2:T(8,128)} %fusion.50, f32[16,1024,48]{1,2,0:T(8,128)} %fusion.41, f32[16,1024,48]{1,2,0:T(8,128)} %fusion.44, bf16[16,48,16]{2,0,1:T(8,128)(2,1)S(1)} %copy.97, f32[1024,16]{0,1:T(8,128)S(1)} %copy-done.7), kind=kOutput, calls=%fused_computation.11 | convolution fusion | flops 29114368 | bytes 14245888 | tf_op jit(solution)/shard_map/tvh,dh->vtd/dot_general | solution.py:41
  132.0 3.2 %fusion.6 = f32[48,4,1024]{2,1,0:T(4,128)S(1)} fusion(bf16[48,16,1024]{2,1,0:T(8,128)(2,1)S(1)} %fusion.8, f32[48,16,1024]{2,1,0:T(8,128)S(1)} %copy-done.3, f32[48,1024]{1,0:T(8,128)S(1)} %copy-done.11, bf16[48,4,16]{2,1,0:T(4,128)(2,1)S(1)} %copy-done.13, pred[48]{0:T(512)(128)(4,1)S(1)} %copy-done.19), kind=kOutput, calls=%fused_computation.9 | convolution fusion | flops 46402560 | bytes 5707824 | tf_op jit(solution)/shard_map/vpt,vtd->vpd/dot_general | solution.py:113
  135.6 2.0 %gather_fusion.1 = f32[72,4096]{1,0:T(8,128)} fusion(f32[48,4096]{1,0:T(8,128)S(1)} %bitcast.108, s32[1024]{0:T(1024)S(1)} %pad_clamp_fusion), kind=kCustom, calls=%fused_computation.1 | custom fusion | bytes 2359584 | tf_op jit(solution)/shard_map/jit(_take)/gather | solution.py:119
  140.4 4.3 %all-to-all-start.2 = ((f32[8,32,9,128]{3,1,2,0:T(8,128)}), f32[8,32,9,128]{3,1,2,0:T(8,128)}, u32[]{:S(2)}, u32[]{:S(2)}) async-start(f32[8,32,9,128]{3,1,2,0:T(8,128)} %select_bitcast_fusion), calls=%async_computation.2 | async-start | bytes 2359296 | tf_op jit(solution)/shard_map/all_to_all | solution.py:121
  144.7 3.2 %subtract_convert_fusion.1 = (bf16[16,16,1024]{2,1,0:T(8,128)(2,1)S(1)}, bf16[16,16,1024]{2,1,0:T(8,128)(2,1)S(1)}) fusion(bf16[16,48,16]{1,2,0:T(8,128)(2,1)S(1)} %copy-done.9, bf16[48,16,1024]{2,1,0:T(8,128)(2,1)} %copy-done.1), kind=kOutput, calls=%fused_computation.44 | convolution fusion | flops 26214400 | bytes 2646016 | tf_op jit(solution)/shard_map/tvh,vtd->thd/dot_general | solution.py:41
  148.5 13.6 %all-to-all-done.2 = f32[8,32,9,128]{3,1,2,0:T(8,128)} async-done(((f32[8,32,9,128]{3,1,2,0:T(8,128)}), f32[8,32,9,128]{3,1,2,0:T(8,128)}, u32[]{:S(2)}, u32[]{:S(2)}) %all-to-all-start.2) | async-done | bytes 1179680 | tf_op jit(solution)/shard_map/all_to_all | solution.py:121
  164.3 5.8 %all-to-all-start.3 = ((f32[32,9,128]{2,1,0:T(8,128)}), f32[32,9,128]{2,1,0:T(8,128)S(1)}, u32[]{:S(2)}, u32[]{:S(2)}) async-start(f32[32,9,128]{2,1,0:T(8,128)} %copy.98), calls=%async_computation.3 | async-start | bytes 524288 | tf_op jit(solution)/shard_map/all_to_all | solution.py:122
  170.9 2.6 %fusion.26 = bf16[16,1024]{1,0:T(8,128)(2,1)} fusion(bf16[16,1024]{1,0:T(8,128)(2,1)S(1)} %reshape.73, bf16[2,1024,1024]{2,1,0:T(8,128)(2,1)} %all-gather.2.cloned.1.call-done), kind=kOutput, calls=%fused_computation.40 | convolution fusion | flops 33570816 | bytes 2162688 | tf_op jit(solution)/shard_map/dot_general | solution.py:92
  173.5 8.6 %all-to-all-done.3 = f32[32,9,128]{2,1,0:T(8,128)S(1)} async-done(((f32[32,9,128]{2,1,0:T(8,128)}), f32[32,9,128]{2,1,0:T(8,128)S(1)}, u32[]{:S(2)}, u32[]{:S(2)}) %all-to-all-start.3) | async-done | bytes 147488 | tf_op jit(solution)/shard_map/all_to_all | solution.py:122
  (94 shorter events, 31.7 us)
Async XLA Ops:
  7.2 30.9 %copy-start = (bf16[48,4,1024]{2,1,0:T(4,128)(2,1)S(1)}, bf16[48,4,1024]{2,1,0:T(4,128)(2,1)}, u32[]{:S(2)}) copy-start(bf16[48,4,1024]{2,1,0:T(4,128)(2,1)} %param.11) | copy-start | bytes 1179652
  7.2 87.5 %all-gather.2.cloned.1.call-start = ((), (), s32[]{:S(2)}) async-start(), calls=%async_computation.4 | async-start | bytes 4325376 | tf_op jit(solution)/shard_map/all_gather | solution.py:67
  15.8 10.4 %all-to-all-start.1 = ((bf16[8,2,288]{2,1,0:T(2,128)(2,1)}), bf16[8,2,288]{2,1,0:T(2,128)(2,1)S(1)}, u32[]{:S(2)}, u32[]{:S(2)}) async-start(bf16[8,2,288]{2,1,0:T(2,128)(2,1)} %reshape.97), calls=%async_computation.1 | async-start | bytes 24576 | tf_op jit(solution)/shard_map/all_to_all | solution.py:71
  23.0 18.1 %copy-start.18 = (pred[48]{0:T(512)(128)(4,1)}, pred[48]{0:T(512)(128)(4,1)S(1)}, u32[]{:S(2)}) copy-start(pred[48]{0:T(512)(128)(4,1)S(1)} %compare_and_fusion.1) | copy-start | bytes 148
  24.6 22.9 %copy-start.10 = (f32[48,1024]{1,0:T(8,128)}, f32[48,1024]{1,0:T(8,128)S(1)}, u32[]{:S(2)}) copy-start(f32[48,1024]{1,0:T(8,128)S(1)} %convert_element_type.88) | copy-start | bytes 589828
  26.1 20.9 %all-to-all-start = ((f32[32,1,512]{2,1,0:T(1,128)}), f32[32,1,512]{2,1,0:T(1,128)S(1)}, u32[]{:S(2)}, u32[]{:S(2)}) async-start(f32[32,1,512]{2,1,0:T(1,128)} %reshape.99), calls=%async_computation | async-start | bytes 131072 | tf_op jit(solution)/shard_map/all_to_all | solution.py:65
  38.1 8.9 %copy-start.12 = (bf16[48,4,16]{2,1,0:T(4,128)(2,1)}, bf16[48,4,16]{2,1,0:T(4,128)(2,1)S(1)}, u32[]{:S(2)}) copy-start(bf16[48,4,16]{2,1,0:T(4,128)(2,1)S(1)} %gather_fusion) | copy-start | bytes 18436
  41.1 53.6 %copy-start.1 = (bf16[48,16,1024]{2,1,0:T(8,128)(2,1)}, bf16[48,16,1024]{2,1,0:T(8,128)(2,1)S(1)}, u32[]{:S(2)}) copy-start(bf16[48,16,1024]{2,1,0:T(8,128)(2,1)S(1)} %get-tuple-element.11) | copy-start | bytes 4718596
  48.7 46.0 %copy-start.5 = (f32[1024,16]{0,1:T(8,128)}, f32[1024,16]{0,1:T(8,128)S(1)}, u32[]{:S(2)}) copy-start(f32[1024,16]{0,1:T(8,128)S(1)} %reshape.71) | copy-start | bytes 196612
  52.2 48.7 %copy-start.20 = (bf16[16,1024]{1,0:T(8,128)(2,1)S(1)}, bf16[16,1024]{1,0:T(8,128)(2,1)}, u32[]{:S(2)}) copy-start(bf16[16,1024]{1,0:T(8,128)(2,1)} %param.17) | copy-start | bytes 98308
  105.2 4.2 %copy-start.15 = (f32[16,48,16]{1,0,2:T(8,128)S(1)}, f32[16,48,16]{1,0,2:T(8,128)}, u32[]{:S(2)}) copy-start(f32[16,48,16]{1,0,2:T(8,128)} %copy-done.14) | copy-start | bytes 147460
  113.0 3.3 %copy-start.4 = (bf16[16,48,16]{2,0,1:T(8,128)(2,1)S(1)}, bf16[16,48,16]{2,0,1:T(8,128)(2,1)}, u32[]{:S(2)}) copy-start(bf16[16,48,16]{2,0,1:T(8,128)(2,1)} %copy.95) | copy-start | bytes 73732
  113.0 3.3 %copy-start.6 = (f32[1024,16]{0,1:T(8,128)S(1)}, f32[1024,16]{0,1:T(8,128)}, u32[]{:S(2)}) copy-start(f32[1024,16]{0,1:T(8,128)} %copy-done.5) | copy-start | bytes 196612
  113.0 5.6 %copy-start.8 = (bf16[16,48,16]{1,2,0:T(8,128)(2,1)S(1)}, bf16[16,48,16]{1,2,0:T(8,128)(2,1)}, u32[]{:S(2)}) copy-start(bf16[16,48,16]{1,2,0:T(8,128)(2,1)} %fusion.59) | copy-start | bytes 73732
  120.9 2.3 %copy-start.16 = (bf16[16,48,16]{1,2,0:T(8,128)(2,1)S(1)}, bf16[16,48,16]{1,2,0:T(8,128)(2,1)}, u32[]{:S(2)}) copy-start(bf16[16,48,16]{1,2,0:T(8,128)(2,1)} %get-tuple-element.4) | copy-start | bytes 73732
  120.9 2.5 %copy-start.7 = (f32[1024,16]{0,1:T(8,128)S(1)}, f32[1024,16]{0,1:T(8,128)}, u32[]{:S(2)}) copy-start(f32[1024,16]{0,1:T(8,128)} %copy-done.5) | copy-start | bytes 196612
  123.4 8.5 %copy-start.3 = (f32[48,16,1024]{2,1,0:T(8,128)S(1)}, f32[48,16,1024]{2,1,0:T(8,128)}, u32[]{:S(2)}) copy-start(f32[48,16,1024]{2,1,0:T(8,128)} %get-tuple-element.12) | copy-start | bytes 9437188
  123.4 8.5 %copy-start.11 = (f32[48,1024]{1,0:T(8,128)S(1)}, f32[48,1024]{1,0:T(8,128)}, u32[]{:S(2)}) copy-start(f32[48,1024]{1,0:T(8,128)} %copy-done.10) | copy-start | bytes 589828
  123.4 8.5 %copy-start.13 = (bf16[48,4,16]{2,1,0:T(4,128)(2,1)S(1)}, bf16[48,4,16]{2,1,0:T(4,128)(2,1)}, u32[]{:S(2)}) copy-start(bf16[48,4,16]{2,1,0:T(4,128)(2,1)} %copy-done.12) | copy-start | bytes 18436
  123.4 8.5 %copy-start.19 = (pred[48]{0:T(512)(128)(4,1)S(1)}, pred[48]{0:T(512)(128)(4,1)}, u32[]{:S(2)}) copy-start(pred[48]{0:T(512)(128)(4,1)} %copy-done.18) | copy-start | bytes 148
  135.6 3.5 %copy-start.17 = (pred[8,9]{1,0:T(8,128)(4,1)S(1)}, pred[8,9]{1,0:T(8,128)(4,1)}, u32[]{:S(2)}) copy-start(pred[8,9]{1,0:T(8,128)(4,1)} %broadcast_in_dim.69) | copy-start | bytes 220
  137.6 7.1 %copy-start.9 = (bf16[16,48,16]{1,2,0:T(8,128)(2,1)S(1)}, bf16[16,48,16]{1,2,0:T(8,128)(2,1)}, u32[]{:S(2)}) copy-start(bf16[16,48,16]{1,2,0:T(8,128)(2,1)} %fusion.59) | copy-start | bytes 73732
  140.4 21.7 %all-to-all-start.2 = ((f32[8,32,9,128]{3,1,2,0:T(8,128)}), f32[8,32,9,128]{3,1,2,0:T(8,128)}, u32[]{:S(2)}, u32[]{:S(2)}) async-start(f32[8,32,9,128]{3,1,2,0:T(8,128)} %select_bitcast_fusion), calls=%async_computation.2 | async-start | bytes 2359296 | tf_op jit(solution)/shard_map/all_to_all | solution.py:121
  164.3 17.8 %all-to-all-start.3 = ((f32[32,9,128]{2,1,0:T(8,128)}), f32[32,9,128]{2,1,0:T(8,128)S(1)}, u32[]{:S(2)}, u32[]{:S(2)}) async-start(f32[32,9,128]{2,1,0:T(8,128)} %copy.98), calls=%async_computation.3 | async-start | bytes 524288 | tf_op jit(solution)/shard_map/all_to_all | solution.py:122
  (2 other events, 2.1 us)
Sparse Core Ops, SparseCore 0:
  10.6 84.0 all-gather.1
